TPU v7x, 32 devices: a whole 2x2x4 slice. The times are simulated.
32 devices in a mesh: groups: 2 (over y), ctx: 8 (over z, x), tp: 2 (over core).
Axes of the slice: x: 2, y: 2, z: 4, core: 2. Of those that a mesh axis runs over, the one named last changes fastest.
Arguments:
- tokens: bfloat16 [4096, 2688], P(('groups', 'ctx', 'tp')), parts along dimension 0, may hold values from -6 to 6
- output_gradient: bfloat16 [4096, 2688], P(('groups', 'ctx', 'tp')), parts along dimension 0, may hold values from -6 to 6
- document_index: int32 [4096], P(('groups', 'ctx')), parts along dimension 0, may hold values from 0 to 3, never falling along the last dimension, each value on 1 to 1024 neighbouring positions
- real_token_count: int32 [16], P(('groups', 'ctx')), parts along dimension 0, may hold values from 64 to 256, as said below
- input_norm_gain: float32 [2688], replicated, may hold values from 0.1 to 1.9
- query_norm_gain: float32 [128], replicated, may hold values from 0.1 to 1.9
- key_norm_gain: float32 [128], replicated, may hold values from 0.1 to 1.9
- output_norm_gain: float32 [2688], replicated, may hold values from 0.1 to 1.9
- query_projection: bfloat16 [2688, 512], P(None, 'tp'), may hold values from -0.125 to 0.125
- key_projection: bfloat16 [2688, 256], P(None, 'tp'), may hold values from -0.125 to 0.125
- value_projection: bfloat16 [2688, 256], P(None, 'tp'), may hold values from -0.125 to 0.125
- output_projection: bfloat16 [512, 2688], P('tp'), may hold values from -0.25 to 0.25
- adapter_down_maps: bfloat16 [2688, 48], replicated, may hold values from -0.125 to 0.125
- adapter_query_up: bfloat16 [16, 512], P(None, 'tp'), may hold values from -0.375 to 0.375
- adapter_key_up: bfloat16 [16, 256], P(None, 'tp'), may hold values from -0.375 to 0.375
- adapter_value_up: bfloat16 [16, 256], P(None, 'tp'), may hold values from -0.375 to 0.375
- adapter_output_down: bfloat16 [512, 16], P('tp'), may hold values from -0.25 to 0.25
- adapter_output_up: bfloat16 [16, 2688], replicated, may hold values from -0.375 to 0.375
Outputs:
- layer_out: bfloat16 [4096, 2688], P(('groups', 'ctx', 'tp')), parts along dimension 0
- grad_in: bfloat16 [4096, 2688], P(('groups', 'ctx', 'tp')), parts along dimension 0
- grad_down: float32 [5376, 48], P(('groups', 'tp')), parts along dimension 0
- query_up_gradient: float32 [32, 512], P('groups', 'tp'), parts along dimension 0
- key_up_gradient: float32 [32, 256], P('groups', 'tp'), parts along dimension 0
- value_up_gradient: float32 [32, 256], P('groups', 'tp'), parts along dimension 0
- grad_down_out: float32 [1024, 16], P(('groups', 'tp')), parts along dimension 0
- output_up_gradient: float32 [32, 2688], P('groups', 'tp'), parts along dimension 0
There are 2 independent parts, one for each index of `groups`. A program takes and returns all parts, laid end to end along the dimension named above; an argument that names none is the same for every part. Nothing has to cross between parts.
Inputs may be any that keep to these rules, and one draw needn't show every extreme that they name: `document_index`: document numbers never fall along the tokens; a document has 1 to 1024 tokens and one has exactly that many. `real_token_count`: the real tokens of a block come first and the rest is padding; some block is full and some holds 64 real tokens.
All inputs are finite; a program needn't handle non-finite values.
Results may differ from a plain program's by a relative error of at most 0.034.
Values may be sent and summed in bfloat16 or wider, within the bound.
No kernel may reach another device: no remote copies, remote signals or barrier semaphores. Data moves between devices by JAX's collectives and lax.ppermute only.
A program may use at most 64 MiB of HBM per device.

v0:
```python
import jax
import jax.numpy as jnp
from jax import lax
from jax.sharding import PartitionSpec as P

WINDOW = 1024
epsilon = 1e-06
adapter_scale = 2.0
score_scale = 168.0 ** (-0.5)


def passed_along(value, axis, steps):
    count = lax.axis_size(axis)
    leading, last = (max(0, -steps), min(count, count - steps))
    return lax.ppermute(value, axis, [(source, source + steps) for source in range(leading, last)])


def norm_rows(source, gain_vec):
    inverse = lax.rsqrt(jnp.mean(source * source, axis=-1, keepdims=True) + epsilon)
    return source * inverse * gain_vec


def norm_back(source, gain_vec, incoming):
    inverse = lax.rsqrt(jnp.mean(source * source, axis=-1, keepdims=True) + epsilon)
    scaled = source * inverse
    upward = incoming * gain_vec
    return inverse * (upward - scaled * jnp.mean(upward * scaled, axis=-1, keepdims=True))


def matrix_product(first_op, second_op):
    return jnp.dot(first_op, second_op, preferred_element_type=jnp.float32)


def multiply_by_transpose(first_op, second_op):
    return lax.dot_general(
        first_op, second_op, (((1,), (1,)), ((), ())), preferred_element_type=jnp.float32
    )


def transpose_multiply(first_op, second_op):
    return lax.dot_general(
        first_op, second_op, (((0,), (0,)), ((), ())), preferred_element_type=jnp.float32
    )


def window_mask(query_segs, key_codes):
    query_count = query_segs.shape[0]
    key_total = key_codes.shape[0]
    distance = (key_total - query_count + jnp.arange(query_count))[:, None] - jnp.arange(key_total)[
        None, :
    ]
    same_doc = key_codes[None, :] == query_segs[:, None] + 1
    return (distance == 0) | (distance > 0) & (distance < WINDOW) & same_doc


def on_device(
    tokens,
    output_gradient,
    document_index,
    real_token_count,
    input_norm_gain,
    query_norm_gain,
    key_norm_gain,
    output_norm_gain,
    query_projection,
    key_projection,
    value_projection,
    output_projection,
    adapter_down_maps,
    adapter_query_up,
    adapter_key_up,
    adapter_value_up,
    adapter_output_down,
    adapter_output_up,
):
    row_count, model_width = tokens.shape
    shard_len = document_index.shape[0]
    head_dim = key_projection.shape[1]
    adapter_product = adapter_key_up.shape[0]
    heads_here = query_projection.shape[1] // head_dim
    ctx_size = lax.axis_size("ctx")
    tp_index = lax.axis_index("tp")
    slice_width = model_width // lax.axis_size("tp")
    reach_shards = WINDOW // shard_len
    send_count = min(reach_shards, ctx_size - 1)
    tok_float = tokens.astype(jnp.float32)
    normed_rows = norm_rows(tok_float, input_norm_gain).astype(jnp.bfloat16)
    normalized_input = lax.all_gather(normed_rows, "tp", axis=0, tiled=True)
    middle_list = matrix_product(normalized_input, adapter_down_maps).astype(jnp.bfloat16)
    middle_query = middle_list[:, :adapter_product]
    middle_key = middle_list[:, adapter_product : 2 * adapter_product]
    middle_value = middle_list[:, 2 * adapter_product :]
    query_before_norm = matrix_product(
        normalized_input, query_projection
    ) + adapter_scale * matrix_product(middle_query, adapter_query_up)
    key_before_norm = matrix_product(
        normalized_input, key_projection
    ) + adapter_scale * matrix_product(middle_key, adapter_key_up)
    value_before_norm = matrix_product(
        normalized_input, value_projection
    ) + adapter_scale * matrix_product(middle_value, adapter_value_up)
    query_heads = query_before_norm.reshape(shard_len, heads_here, head_dim)
    query_normed = norm_rows(query_heads, query_norm_gain).astype(jnp.bfloat16)
    key_normed = norm_rows(key_before_norm, key_norm_gain).astype(jnp.bfloat16)
    value_cast = value_before_norm.astype(jnp.bfloat16)
    positions = jnp.arange(shard_len)
    is_valid = positions < real_token_count[0]
    valid_rows = is_valid.astype(jnp.float32)
    local_codes = jnp.where(is_valid, document_index + 1, 0)
    local_pair = jnp.concatenate([key_normed, value_cast], axis=1)
    received = []
    for hop_index in range(1, send_count + 1):
        received.append(passed_along((local_pair, local_codes), "ctx", hop_index))
    missing = reach_shards - send_count
    blank_pair = jnp.zeros_like(local_pair)
    blank_codes = jnp.zeros_like(local_codes)
    earlier = [(blank_pair, blank_codes)] * missing + list(reversed(received))
    key_pairs = jnp.concatenate([entry[0] for entry in earlier] + [local_pair], axis=0)
    key_codes_all = jnp.concatenate([entry[1] for entry in earlier] + [local_codes], axis=0)
    keys_all = key_pairs[:, :head_dim]
    values_all = key_pairs[:, head_dim:]
    allowed = window_mask(document_index, key_codes_all)
    scores = (
        jnp.einsum("thd,sd->hts", query_normed, keys_all, preferred_element_type=jnp.float32)
        * score_scale
    )
    weights = jnp.where(allowed[None], jnp.exp(scores), 0.0)
    attn_probs = weights / jnp.sum(weights, axis=-1, keepdims=True)
    probs_cast = attn_probs.astype(jnp.bfloat16)
    attention_result = jnp.einsum(
        "hts,sd->thd", probs_cast, values_all, preferred_element_type=jnp.float32
    )
    attention_result = (
        (attention_result * valid_rows[:, None, None])
        .astype(jnp.bfloat16)
        .reshape(shard_len, heads_here * head_dim)
    )
    part_out = matrix_product(attention_result, output_projection)
    partial_middle = matrix_product(attention_result, adapter_output_down)
    output_total, mid_sum = (
        lax.psum_scatter(
            part_out.astype(jnp.bfloat16), "tp", scatter_dimension=0, tiled=True
        ).astype(jnp.float32),
        lax.psum_scatter(
            partial_middle.astype(jnp.bfloat16), "tp", scatter_dimension=0, tiled=True
        ).astype(jnp.float32),
    )
    middle_output = mid_sum.astype(jnp.bfloat16)
    apply_prenorm = output_total + adapter_scale * matrix_product(middle_output, adapter_output_up)
    layer_out = norm_rows(apply_prenorm, output_norm_gain).astype(jnp.bfloat16)
    prenorm_gradient = norm_back(
        apply_prenorm, output_norm_gain, output_gradient.astype(jnp.float32)
    ).astype(jnp.bfloat16)
    middle_output_gradient = (
        adapter_scale * multiply_by_transpose(prenorm_gradient, adapter_output_up)
    ).astype(jnp.bfloat16)
    complete_gradient, middle_complete_gradient, middle_complete = (
        lax.all_gather(prenorm_gradient, "tp", axis=0, tiled=True),
        lax.all_gather(middle_output_gradient, "tp", axis=0, tiled=True),
        lax.all_gather(middle_output, "tp", axis=0, tiled=True),
    )
    gradient_portion = lax.dynamic_slice_in_dim(
        complete_gradient, tp_index * slice_width, slice_width, 1
    )
    output_up_contribution = adapter_scale * transpose_multiply(middle_complete, gradient_portion)
    attention_gradient = multiply_by_transpose(
        complete_gradient, output_projection
    ) + multiply_by_transpose(middle_complete_gradient, adapter_output_down)
    attention_gradient = (attention_gradient * valid_rows[:, None]).astype(jnp.bfloat16)
    down_out_term = transpose_multiply(attention_result, middle_complete_gradient)
    grad_heads = attention_gradient.reshape(shard_len, heads_here, head_dim)
    grad_probs = jnp.einsum(
        "thd,sd->hts", grad_heads, values_all, preferred_element_type=jnp.float32
    )
    inner_sum = jnp.sum(attn_probs * grad_probs, axis=-1, keepdims=True)
    grad_scores = (attn_probs * (grad_probs - inner_sum) * score_scale).astype(jnp.bfloat16)
    grad_query = jnp.einsum(
        "hts,sd->thd", grad_scores, keys_all, preferred_element_type=jnp.float32
    )
    grad_keys = jnp.einsum(
        "hts,thd->sd", grad_scores, query_normed, preferred_element_type=jnp.float32
    )
    grad_values = jnp.einsum(
        "hts,thd->sd", probs_cast, grad_heads, preferred_element_type=jnp.float32
    )
    grad_pairs = jnp.concatenate([grad_keys, grad_values], axis=1)
    own_grads = grad_pairs[reach_shards * shard_len :]
    for hop_index in range(1, send_count + 1):
        own_grads = own_grads + passed_along(
            grad_pairs[
                (reach_shards - hop_index) * shard_len : (reach_shards - hop_index + 1) * shard_len
            ].astype(jnp.bfloat16),
            "ctx",
            -hop_index,
        ).astype(jnp.float32)
    query_prenorm_gradient = (
        norm_back(query_heads, query_norm_gain, grad_query)
        .reshape(shard_len, heads_here * head_dim)
        .astype(jnp.bfloat16)
    )
    key_prenorm_gradient = norm_back(
        key_before_norm, key_norm_gain, own_grads[:, :head_dim]
    ).astype(jnp.bfloat16)
    value_prenorm_gradient = own_grads[:, head_dim:].astype(jnp.bfloat16)
    query_up_contribution = adapter_scale * transpose_multiply(middle_query, query_prenorm_gradient)
    key_up_contribution = adapter_scale * transpose_multiply(middle_key, key_prenorm_gradient)
    value_up_contribution = adapter_scale * transpose_multiply(middle_value, value_prenorm_gradient)
    middle_gradients = jnp.concatenate(
        [
            adapter_scale * multiply_by_transpose(query_prenorm_gradient, adapter_query_up),
            adapter_scale * multiply_by_transpose(key_prenorm_gradient, adapter_key_up),
            adapter_scale * multiply_by_transpose(value_prenorm_gradient, adapter_value_up),
        ],
        axis=1,
    ).astype(jnp.bfloat16)
    grad_normed = (
        multiply_by_transpose(query_prenorm_gradient, query_projection)
        + multiply_by_transpose(key_prenorm_gradient, key_projection)
        + multiply_by_transpose(value_prenorm_gradient, value_projection)
        + multiply_by_transpose(middle_gradients, adapter_down_maps)
    )
    grad_normed_rows = lax.psum_scatter(
        grad_normed.astype(jnp.bfloat16), "tp", scatter_dimension=0, tiled=True
    ).astype(jnp.float32)
    grad_in = norm_back(tok_float, input_norm_gain, grad_normed_rows).astype(jnp.bfloat16)
    down_term = lax.psum_scatter(
        transpose_multiply(normalized_input, middle_gradients).astype(jnp.bfloat16),
        "tp",
        scatter_dimension=0,
        tiled=True,
    )
    adapter_totals = (
        lax.psum(down_term, "ctx").astype(jnp.float32),
        lax.psum(query_up_contribution.astype(jnp.bfloat16), "ctx").astype(jnp.float32),
        lax.psum(key_up_contribution.astype(jnp.bfloat16), "ctx").astype(jnp.float32),
        lax.psum(value_up_contribution.astype(jnp.bfloat16), "ctx").astype(jnp.float32),
        lax.psum(down_out_term.astype(jnp.bfloat16), "ctx").astype(jnp.float32),
        lax.psum(output_up_contribution.astype(jnp.bfloat16), "ctx").astype(jnp.float32),
    )
    return (
        layer_out,
        grad_in,
        adapter_totals[0],
        adapter_totals[1],
        adapter_totals[2],
        adapter_totals[3],
        adapter_totals[4],
        adapter_totals[5],
    )


def solution(mesh):
    in_specs = (
        P(("groups", "ctx", "tp"), None),
        P(("groups", "ctx", "tp"), None),
        P(("groups", "ctx")),
        P(("groups", "ctx")),
        P(),
        P(),
        P(),
        P(),
        P(None, "tp"),
        P(None, "tp"),
        P(None, "tp"),
        P("tp", None),
        P(),
        P(None, "tp"),
        P(None, "tp"),
        P(None, "tp"),
        P("tp", None),
        P(),
    )
    out_specs = (
        P(("groups", "ctx", "tp"), None),
        P(("groups", "ctx", "tp"), None),
        P(("groups", "tp"), None),
        P("groups", "tp"),
        P("groups", "tp"),
        P("groups", "tp"),
        P(("groups", "tp"), None),
        P("groups", "tp"),
    )
    return jax.shard_map(
        on_device, mesh=mesh, in_specs=in_specs, out_specs=out_specs, check_vma=False
    )
```

profile of v0, /device:TPU:0, one launch (start us, length us, event | category | flops | bytes accessed | tf_op | source)
XLA Modules:
  0.0 319.8 jit_solution(16461796081767223556)
XLA Ops:
  7.2 1.4 fusion.26
  9.2 2.2 fusion.21
  12.2 5.9 %collective-permute-start.4 = (s32[256]{0:T(256)S(1)}, s32[256]{0:T(256)S(1)}, u32[]{:S(2)}, u32[]{:S(2)}) collective-permute-start(s32[256]{0:T(256)S(1)} %get-tuple-element.19), channel_id=1, source_target_pairs={{0,8},{2,10},{4,12},{6,14},{1,9},{3,11},{5,13},{7,15},{16,24},{18,... | collective-permute-start | bytes 3080 | tf_op jit(solution)/shard_map/ppermute | solution.py:15
  18.1 4.4 %collective-permute-start.5 = (s32[256]{0:T(256)S(1)}, s32[256]{0:T(256)S(1)}, u32[]{:S(2)}, u32[]{:S(2)}) collective-permute-start(s32[256]{0:T(256)S(1)} %get-tuple-element.19), channel_id=1, source_target_pairs={{0,6},{2,8},{4,10},{6,12},{8,14},{1,7},{3,9},{5,11},{7,13},{9,15},... | collective-permute-start | bytes 3080 | tf_op jit(solution)/shard_map/ppermute | solution.py:15
  22.5 1.3 collective-permute-start.6
  23.8 3.1 collective-permute-start.7
  27.0 1.2 collective-permute-done.7
  28.2 1.3 fusion.35
  29.5 2.0 convolution_convert_fusion.2
  33.5 3.9 %collective-permute-start = (bf16[256,256]{0,1:T(8,128)(2,1)S(1)}, bf16[256,256]{0,1:T(8,128)(2,1)S(1)}, u32[]{:S(2)}, u32[]{:S(2)}) collective-permute-start(bf16[256,256]{0,1:T(8,128)(2,1)S(1)} %pad_maximum_fusion.1), channel_id=1, source_target_pairs={{0,8},{2,10},{4,12},{6,14},{1,9},{3,11},{5,13},{7,15},{16,24},{18,... | collective-permute-start | bytes 393224 | tf_op jit(solution)/shard_map/ppermute | solution.py:15
  37.4 1.3 collective-permute-start.1
  38.7 1.9 collective-permute-start.2
  40.5 2.8 collective-permute-start.3
  44.4 0.7 constant_dynamic-update-slice_fusion.4
  45.8 0.7 constant_dynamic-update-slice_fusion.2
  47.2 0.7 constant_dynamic-update-slice_fusion
  47.9 3.4 %fusion.31 = f32[2,256,1280]{1,2,0:T(8,128)} fusion(pred[256,1280]{0,1:T(8,128)(4,1)S(1)} %copy-done.21, bf16[1280,256]{0,1:T(8,128)(2,1)} %constant_dynamic-update-slice_fusion, f32[256,256]{0,1:T(8,128)S(1)} %get-tuple-element.24, f32[128]{0:T(128)S(1)} %copy-done.43, f32[256,2]{0,1:T(2,128)S(1)} %add_rsqrt_fusion), kind=kOutput, calls=%fused_computation.49 | convolution fusion | flops 169936640 | bytes 3541504 | tf_op jit(solution)/shard_map/div | solution.py:128
  51.3 2.2 fusion.46
  53.7 0.8 copy.52
  54.5 3.0 convolution_convert_fusion
  57.6 8.8 %reduce-scatter.13.cloned.1.call-done = bf16[128,16]{1,0:T(8,128)(2,1)} async-done(((bf16[256,16]{1,0:T(8,128)(2,1)}), bf16[128,16]{1,0:T(8,128)(2,1)}) %reduce-scatter.13.cloned.1.call-update) | async-done | bytes 4112
  66.4 12.3 %reduce-scatter.9.cloned.1.call-done = bf16[128,2688]{1,0:T(8,128)(2,1)} async-done(((bf16[256,2688]{1,0:T(8,128)(2,1)}), bf16[128,2688]{1,0:T(8,128)(2,1)}) %reduce-scatter.9.cloned.1.call-update) | async-done | bytes 688144 | tf_op jit(solution)/shard_map/reduce_scatter | solution.py:141
  78.6 1.6 multiply_reduce_fusion.2
  80.6 1.5 multiply_convert_fusion
  82.2 0.8 copy.53
  83.1 1.8 all_gather.15
  84.9 1.4 fusion.52
  86.2 1.9 all_gather.14
  88.1 0.8 convolution_convert_fusion.4
  89.1 4.0 %all-gather.5.cloned.1.call-done = bf16[256,2688]{1,0:T(8,128)(2,1)} async-done(((bf16[128,2688]{1,0:T(8,128)(2,1)}), bf16[256,2688]{1,0:T(8,128)(2,1)}) %all-gather.5.cloned.1.call-update) | async-done | bytes 1376272 | tf_op jit(solution)/shard_map/all_gather | solution.py:158
  93.1 2.3 fusion.45
  95.4 3.2 convolution_bitcast_fusion
  99.3 5.7 %multiply_reduce_fusion.3 = (f32[256,2]{0,1:T(2,128)S(1)}, f32[256,2,128]{0,2,1:T(8,128)}) fusion(f32[256,256]{0,1:T(8,128)} %copy-done.18, f32[256,2]{0,1:T(2,128)S(1)} %copy-done.37, f32[128]{0:T(128)S(1)} %copy-done.44, f32[2,256,1280]{1,2,0:T(8,128)} %fusion.31, f32[2,256,1280]{1,2,0:T(8,128)} %convolution_bitcast_fusion, ...), kind=kOutput, calls=%fused_computation.99 | convolution fusion | flops 171312384 | bytes 11342336 | tf_op jit(solution)/shard_map/hts,sd->thd/dot_general | solution.py:177
  105.0 5.7 %convolution_bitcast_fusion.2 = f32[1280,128]{0,1:T(8,128)} fusion(f32[2,256,1280]{1,2,0:T(8,128)} %fusion.31, f32[2,256,1280]{1,2,0:T(8,128)} %convolution_bitcast_fusion, f32[256,256]{0,1:T(8,128)} %copy-done.18, f32[128]{0:T(128)S(1)} %copy-done.44, f32[256,2]{0,1:T(2,128)S(1)} %copy-done.37), kind=kOutput, calls=%fused_computation.19 | convolution fusion | flops 171247360 | bytes 6162944 | tf_op jit(solution)/shard_map/hts,thd->sd/dot_general | solution.py:180
  110.7 1.1 multiply_convert_fusion.2
  111.8 0.8 fusion.48
  112.7 2.1 fusion.83
  115.0 1.4 collective-permute-start.10
  116.4 1.3 collective-permute-start.11
  117.7 1.3 collective-permute-start.8
  119.0 1.6 collective-permute-start.9
  120.6 1.0 fusion.12
  121.7 2.0 collective-permute-done.10
  123.7 10.1 %collective-permute-done.11 = bf16[256,256]{0,1:T(8,128)(2,1)S(1)} collective-permute-done((bf16[256,256]{0,1:T(8,128)(2,1)S(1)}, bf16[256,256]{0,1:T(8,128)(2,1)S(1)}, u32[]{:S(2)}, u32[]{:S(2)}) %collective-permute-start.11) | collective-permute-done | bytes 131104 | tf_op jit(solution)/shard_map/ppermute | solution.py:15
  134.1 0.7 fusion.54
  135.8 1.1 convolution_convert_fusion.1
  136.9 2.1 copy.54
  139.0 0.7 fusion.53
  139.8 3.9 %convolution_add_fusion.1 = f32[256,2688]{1,0:T(8,128)} fusion(f32[256,2688]{1,0:T(8,128)} %fusion.83, bf16[256,128]{0,1:T(8,128)(2,1)S(1)} %multiply_convert_fusion.4, bf16[2688,128]{1,0:T(8,128)(2,1)S(1)} %copy-done.8), kind=kOutput, calls=%fused_computation.2 | convolution fusion | flops 176848896 | bytes 6258688 | tf_op jit(solution)/shard_map/dot_general | solution.py:35
  143.8 2.1 fusion.63
  145.9 3.6 %reduce-scatter.15.cloned.1.call-done = bf16[1344,48]{1,0:T(8,128)(2,1)} async-done(((bf16[2688,48]{1,0:T(8,128)(2,1)}), bf16[1344,48]{1,0:T(8,128)(2,1)}) %reduce-scatter.15.cloned.1.call-update) | async-done | bytes 129040
  149.5 1.8 copy.55
  151.4 4.3 %fusion.2 = bf16[256,2688]{1,0:T(8,128)(2,1)} fusion(f32[256,2688]{1,0:T(8,128)} %fusion.63, f32[256,2688]{1,0:T(8,128)} %convolution_add_fusion.1, bf16[2688,128]{1,0:T(8,128)(2,1)S(1)} %copy-done.12, f32[256,256]{0,1:T(8,128)S(1)} %copy-done.5), kind=kOutput, calls=%fused_computation.5 | convolution fusion | flops 178225152 | bytes 7634944 | tf_op jit(solution)/shard_map/dot_general | solution.py:35
  155.7 70.0 %all-reduce.6.cloned.1.call-done = (bf16[16,256]{1,0:T(8,128)(2,1)}, bf16[16,128]{1,0:T(8,128)(2,1)}, bf16[16,128]{1,0:T(8,128)(2,1)}, bf16[256,16]{0,1:T(8,128)(2,1)}, bf16[16,1344]{1,0:T(8,128)(2,1)}) async-done(((bf16[16,256]{1,0:T(8,128)(2,1)}, bf16[16,128]{1,0:T(8,128)(2,1)}, bf16[16,128]{1,0:T(8,128)(2,1)}, bf16[256,16]{0,1:T(8,128)(2,1)}, bf16[16,1344]{1,0:T(8,128)(2,1)}), ...) | async-done | bytes 67600 | tf_op jit(solution)/shard_map/psum | solution.py:234
  225.7 1.4 convert_element_type.179
  227.1 1.3 convert_element_type.171
  228.4 1.3 convert_element_type.177
  229.7 1.3 convert_element_type.173
  231.0 1.3 convert_element_type.175
  232.3 67.5 %all-reduce.4.cloned.1.call-done = bf16[1344,48]{0,1:T(8,128)(2,1)} async-done(((bf16[1344,48]{0,1:T(8,128)(2,1)}), bf16[1344,48]{0,1:T(8,128)(2,1)}) %all-reduce.4.cloned.1.call-update) | async-done | bytes 129040 | tf_op jit(solution)/shard_map/psum | solution.py:233
  299.8 1.6 convert_element_type.169
  301.4 8.7 %reduce-scatter.11.cloned.1.call-done = bf16[128,2688]{1,0:T(8,128)(2,1)} async-done(((bf16[256,2688]{1,0:T(8,128)(2,1)}), bf16[128,2688]{1,0:T(8,128)(2,1)}) %reduce-scatter.11.cloned.1.call-update) | async-done | bytes 688144 | tf_op jit(solution)/shard_map/reduce_scatter | solution.py:222
  310.1 1.6 fusion.22
  311.7 1.3 fusion.25
  (155 shorter events, 8.1 us)
Async XLA Ops:
  7.2 36.4 %copy-start = (bf16[2688,256]{1,0:T(8,128)(2,1)S(1)}, bf16[2688,256]{1,0:T(8,128)(2,1)}, u32[]{:S(2)}) copy-start(bf16[2688,256]{1,0:T(8,128)(2,1)} %param.26) | copy-start | bytes 4128772
  7.2 5.0 %copy-start.42 = (s32[256]{0:T(256)S(1)}, s32[256]{0:T(256)}, u32[]{:S(2)}) copy-start(s32[256]{0:T(256)} %param.20) | copy-start | bytes 3076
  7.2 22.3 %all-gather.3.cloned.1.call-start = ((), (), s32[]{:S(2)}) async-start(), calls=%async_computation.4 | async-start | bytes 2064384 | tf_op jit(solution)/shard_map/all_gather | solution.py:88
  11.4 20.2 %copy-start.32 = (bf16[16,128]{1,0:T(8,128)(2,1)S(1)}, bf16[16,128]{1,0:T(8,128)(2,1)}, u32[]{:S(2)}) copy-start(bf16[16,128]{1,0:T(8,128)(2,1)} %param.32) | copy-start | bytes 12292
  11.4 20.4 %copy-start.7 = (bf16[2688,128]{1,0:T(8,128)(2,1)S(1)}, bf16[2688,128]{1,0:T(8,128)(2,1)}, u32[]{:S(2)}) copy-start(bf16[2688,128]{1,0:T(8,128)(2,1)} %param.27) | copy-start | bytes 2064388
  11.4 55.0 %reduce-scatter.13.cloned.1.call-start = ((), (), s32[]{:S(2)}) async-start(), calls=%async_computation.9 | async-start | bytes 98304
  12.2 14.8 %collective-permute-start.4 = (s32[256]{0:T(256)S(1)}, s32[256]{0:T(256)S(1)}, u32[]{:S(2)}, u32[]{:S(2)}) collective-permute-start(s32[256]{0:T(256)S(1)} %get-tuple-element.19), channel_id=1, source_target_pairs={{0,8},{2,10},{4,12},{6,14},{1,9},{3,11},{5,13},{7,15},{16,24},{18,... | collective-permute-start | bytes 3080 | tf_op jit(solution)/shard_map/ppermute | solution.py:15
  18.1 8.9 %collective-permute-start.5 = (s32[256]{0:T(256)S(1)}, s32[256]{0:T(256)S(1)}, u32[]{:S(2)}, u32[]{:S(2)}) collective-permute-start(s32[256]{0:T(256)S(1)} %get-tuple-element.19), channel_id=1, source_target_pairs={{0,6},{2,8},{4,10},{6,12},{8,14},{1,7},{3,9},{5,11},{7,13},{9,15},... | collective-permute-start | bytes 3080 | tf_op jit(solution)/shard_map/ppermute | solution.py:15
  22.5 4.5 %collective-permute-start.6 = (s32[256]{0:T(256)S(1)}, s32[256]{0:T(256)S(1)}, u32[]{:S(2)}, u32[]{:S(2)}) collective-permute-start(s32[256]{0:T(256)S(1)} %get-tuple-element.19), channel_id=1, source_target_pairs={{0,4},{2,6},{4,8},{6,10},{8,12},{10,14},{1,5},{3,7},{5,9},{7,11},{... | collective-permute-start | bytes 3080 | tf_op jit(solution)/shard_map/ppermute | solution.py:15
  23.8 4.4 %collective-permute-start.7 = (s32[256]{0:T(256)S(1)}, s32[256]{0:T(256)S(1)}, u32[]{:S(2)}, u32[]{:S(2)}) collective-permute-start(s32[256]{0:T(256)S(1)} %get-tuple-element.19), channel_id=1, source_target_pairs={{0,2},{2,4},{4,6},{6,8},{8,10},{10,12},{12,14},{1,3},{3,5},{5,7},{... | collective-permute-start | bytes 3080 | tf_op jit(solution)/shard_map/ppermute | solution.py:15
  27.0 24.3 %copy-start.34 = (f32[256]{0:T(256)}, f32[256]{0:T(256)S(1)}, u32[]{:S(2)}) copy-start(f32[256]{0:T(256)S(1)} %fusion.70) | copy-start | bytes 3076
  29.5 2.3 copy-start.1
  31.5 0.9 copy-start.30
  31.5 1.2 copy-start.40
  31.5 1.2 copy-start.11
  32.4 1.0 copy-start.14
  32.7 10.7 %copy-start.28 = (bf16[16,256]{1,0:T(8,128)(2,1)S(1)}, bf16[16,256]{1,0:T(8,128)(2,1)}, u32[]{:S(2)}) copy-start(bf16[16,256]{1,0:T(8,128)(2,1)} %param.31) | copy-start | bytes 24580
  33.5 10.9 %collective-permute-start = (bf16[256,256]{0,1:T(8,128)(2,1)S(1)}, bf16[256,256]{0,1:T(8,128)(2,1)S(1)}, u32[]{:S(2)}, u32[]{:S(2)}) collective-permute-start(bf16[256,256]{0,1:T(8,128)(2,1)S(1)} %pad_maximum_fusion.1), channel_id=1, source_target_pairs={{0,8},{2,10},{4,12},{6,14},{1,9},{3,11},{5,13},{7,15},{16,24},{18,... | collective-permute-start | bytes 393224 | tf_op jit(solution)/shard_map/ppermute | solution.py:15
  37.4 7.7 %collective-permute-start.1 = (bf16[256,256]{0,1:T(8,128)(2,1)S(1)}, bf16[256,256]{0,1:T(8,128)(2,1)S(1)}, u32[]{:S(2)}, u32[]{:S(2)}) collective-permute-start(bf16[256,256]{0,1:T(8,128)(2,1)S(1)} %pad_maximum_fusion.1), channel_id=1, source_target_pairs={{0,6},{2,8},{4,10},{6,12},{8,14},{1,7},{3,9},{5,11},{7,13},{9,15},... | collective-permute-start | bytes 393224 | tf_op jit(solution)/shard_map/ppermute | solution.py:15
  38.7 7.1 %collective-permute-start.2 = (bf16[256,256]{0,1:T(8,128)(2,1)S(1)}, bf16[256,256]{0,1:T(8,128)(2,1)S(1)}, u32[]{:S(2)}, u32[]{:S(2)}) collective-permute-start(bf16[256,256]{0,1:T(8,128)(2,1)S(1)} %pad_maximum_fusion.1), channel_id=1, source_target_pairs={{0,4},{2,6},{4,8},{6,10},{8,12},{10,14},{1,5},{3,7},{5,9},{7,11},{... | collective-permute-start | bytes 393224 | tf_op jit(solution)/shard_map/ppermute | solution.py:15
  40.5 5.9 %collective-permute-start.3 = (bf16[256,256]{0,1:T(8,128)(2,1)S(1)}, bf16[256,256]{0,1:T(8,128)(2,1)S(1)}, u32[]{:S(2)}, u32[]{:S(2)}) collective-permute-start(bf16[256,256]{0,1:T(8,128)(2,1)S(1)} %pad_maximum_fusion.1), channel_id=1, source_target_pairs={{0,2},{2,4},{4,6},{6,8},{8,10},{10,12},{12,14},{1,3},{3,5},{5,7},{... | collective-permute-start | bytes 393224 | tf_op jit(solution)/shard_map/ppermute | solution.py:15
  43.6 4.3 %copy-start.21 = (pred[256,1280]{0,1:T(8,128)(4,1)S(1)}, pred[256,1280]{0,1:T(8,128)(4,1)}, u32[]{:S(2)}) copy-start(pred[256,1280]{0,1:T(8,128)(4,1)} %fusion.35) | copy-start | bytes 983044
  43.6 4.2 %copy-start.43 = (f32[128]{0:T(128)S(1)}, f32[128]{0:T(128)}, u32[]{:S(2)}) copy-start(f32[128]{0:T(128)} %param.23) | copy-start | bytes 1540
  44.3 3.5 %copy-start.18 = (f32[256,256]{0,1:T(8,128)}, f32[256,256]{0,1:T(8,128)S(1)}, u32[]{:S(2)}) copy-start(f32[256,256]{0,1:T(8,128)S(1)} %get-tuple-element.24) | copy-start | bytes 786436
  44.3 6.9 %copy-start.36 = (f32[256,2]{0,1:T(2,128)}, f32[256,2]{0,1:T(2,128)S(1)}, u32[]{:S(2)}) copy-start(f32[256,2]{0,1:T(2,128)S(1)} %add_rsqrt_fusion) | copy-start | bytes 6148
  51.3 2.2 copy-start.26
  53.5 4.0 %copy-start.16 = (bf16[128,2,256]{2,0,1:T(8,128)(2,1)}, bf16[128,2,256]{2,0,1:T(8,128)(2,1)S(1)}, u32[]{:S(2)}) copy-start(bf16[128,2,256]{2,0,1:T(8,128)(2,1)S(1)} %fusion.46) | copy-start | bytes 393220
  54.4 24.2 %reduce-scatter.9.cloned.1.call-start = ((), (), s32[]{:S(2)}) async-start(), calls=%async_computation.5 | async-start | bytes 2064384 | tf_op jit(solution)/shard_map/reduce_scatter | solution.py:141
  57.5 21.2 %copy-start.20 = (bf16[16,2688]{1,0:T(8,128)(2,1)S(1)}, bf16[16,2688]{1,0:T(8,128)(2,1)}, u32[]{:S(2)}) copy-start(bf16[16,2688]{1,0:T(8,128)(2,1)} %param.35) | copy-start | bytes 258052
  57.5 22.7 %copy-start.9 = (bf16[128,2688]{1,0:T(8,128)(2,1)S(1)}, bf16[128,2688]{1,0:T(8,128)(2,1)}, u32[]{:S(2)}) copy-start(bf16[128,2688]{1,0:T(8,128)(2,1)} %param.19) | copy-start | bytes 2064388
  57.5 35.6 %all-gather.5.cloned.1.call-start = ((), (), s32[]{:S(2)}) async-start(), calls=%async_computation.6 | async-start | bytes 2064384 | tf_op jit(solution)/shard_map/all_gather | solution.py:158
  78.6 1.6 copy-start.25
  82.1 5.9 %copy-start.17 = (bf16[128,2,256]{2,0,1:T(8,128)(2,1)S(1)}, bf16[128,2,256]{2,0,1:T(8,128)(2,1)}, u32[]{:S(2)}) copy-start(bf16[128,2,256]{2,0,1:T(8,128)(2,1)} %copy-done.16) | copy-start | bytes 393220
  82.1 6.7 %copy-start.27 = (bf16[256,16]{0,1:T(8,128)(2,1)S(1)}, bf16[256,16]{0,1:T(8,128)(2,1)}, u32[]{:S(2)}) copy-start(bf16[256,16]{0,1:T(8,128)(2,1)} %param.34) | copy-start | bytes 24580
  82.1 10.9 %copy-start.35 = (f32[256]{0:T(256)S(1)}, f32[256]{0:T(256)}, u32[]{:S(2)}) copy-start(f32[256]{0:T(256)} %copy-done.34) | copy-start | bytes 3076
  82.2 67.3 %reduce-scatter.15.cloned.1.call-start = ((), (), s32[]{:S(2)}) async-start(), calls=%async_computation.10 | async-start | bytes 1032192
  95.4 3.2 copy-start.3
  98.6 0.7 copy-start.37
  98.6 0.7 copy-start.44
  105.0 7.6 %copy-start.29 = (bf16[16,256]{1,0:T(8,128)(2,1)S(1)}, bf16[16,256]{1,0:T(8,128)(2,1)}, u32[]{:S(2)}) copy-start(bf16[16,256]{1,0:T(8,128)(2,1)} %param.31) | copy-start | bytes 24580
  112.7 2.1 copy-start.13
  114.8 5.8 %copy-start.6 = (bf16[256,2688]{1,0:T(8,128)(2,1)S(1)}, bf16[256,2688]{1,0:T(8,128)(2,1)}, u32[]{:S(2)}) copy-start(bf16[256,2688]{1,0:T(8,128)(2,1)} %all-gather.5.cloned.1.call-done) | copy-start | bytes 4128772
  115.0 8.7 %collective-permute-start.10 = (bf16[256,256]{0,1:T(8,128)(2,1)S(1)}, bf16[256,256]{0,1:T(8,128)(2,1)S(1)}, u32[]{:S(2)}, u32[]{:S(2)}) collective-permute-start(bf16[256,256]{0,1:T(8,128)(2,1)S(1)} %get-tuple-element.17), channel_id=1, source_target_pairs={{6,0},{8,2},{10,4},{12,6},{14,8},{7,1},{9,3},{11,5},{13,7},{15,9},... | collective-permute-start | bytes 393224 | tf_op jit(solution)/shard_map/ppermute | solution.py:15
  116.4 17.4 %collective-permute-start.11 = (bf16[256,256]{0,1:T(8,128)(2,1)S(1)}, bf16[256,256]{0,1:T(8,128)(2,1)S(1)}, u32[]{:S(2)}, u32[]{:S(2)}) collective-permute-start(bf16[256,256]{0,1:T(8,128)(2,1)S(1)} %get-tuple-element.16), channel_id=1, source_target_pairs={{8,0},{10,2},{12,4},{14,6},{9,1},{11,3},{13,5},{15,7},{24,16},{26,... | collective-permute-start | bytes 393224 | tf_op jit(solution)/shard_map/ppermute | solution.py:15
  117.7 16.1 %collective-permute-start.8 = (bf16[256,256]{0,1:T(8,128)(2,1)S(1)}, bf16[256,256]{0,1:T(8,128)(2,1)S(1)}, u32[]{:S(2)}, u32[]{:S(2)}) collective-permute-start(bf16[256,256]{0,1:T(8,128)(2,1)S(1)} %get-tuple-element.15), channel_id=1, source_target_pairs={{2,0},{4,2},{6,4},{8,6},{10,8},{12,10},{14,12},{3,1},{5,3},{7,5},{... | collective-permute-start | bytes 393224 | tf_op jit(solution)/shard_map/ppermute | solution.py:15
  119.0 14.9 %copy-start.15 = (f32[256,128]{0,1:T(8,128)S(1)}, f32[256,128]{0,1:T(8,128)}, u32[]{:S(2)}) copy-start(f32[256,128]{0,1:T(8,128)} %copy-done.14) | copy-start | bytes 393220
  119.0 14.9 %copy-start.41 = (f32[128]{0:T(128)S(1)}, f32[128]{0:T(128)}, u32[]{:S(2)}) copy-start(f32[128]{0:T(128)} %param.24) | copy-start | bytes 1540
  119.0 14.8 %collective-permute-start.9 = (bf16[256,256]{0,1:T(8,128)(2,1)S(1)}, bf16[256,256]{0,1:T(8,128)(2,1)S(1)}, u32[]{:S(2)}, u32[]{:S(2)}) collective-permute-start(bf16[256,256]{0,1:T(8,128)(2,1)S(1)} %get-tuple-element.18), channel_id=1, source_target_pairs={{4,0},{6,2},{8,4},{10,6},{12,8},{14,10},{5,1},{7,3},{9,5},{11,7},{... | collective-permute-start | bytes 393224 | tf_op jit(solution)/shard_map/ppermute | solution.py:15
  121.7 13.2 %copy-start.31 = (bf16[16,128]{1,0:T(8,128)(2,1)S(1)}, bf16[16,128]{1,0:T(8,128)(2,1)}, u32[]{:S(2)}) copy-start(bf16[16,128]{1,0:T(8,128)(2,1)} %param.33) | copy-start | bytes 12292
  121.7 13.4 %copy-start.33 = (bf16[16,128]{1,0:T(8,128)(2,1)S(1)}, bf16[16,128]{1,0:T(8,128)(2,1)}, u32[]{:S(2)}) copy-start(bf16[16,128]{1,0:T(8,128)(2,1)} %param.32) | copy-start | bytes 12292
  134.0 1.0 copy-start.4
  135.2 0.6 copy-start.23
  135.8 4.0 %copy-start.8 = (bf16[2688,128]{1,0:T(8,128)(2,1)S(1)}, bf16[2688,128]{1,0:T(8,128)(2,1)}, u32[]{:S(2)}) copy-start(bf16[2688,128]{1,0:T(8,128)(2,1)} %param.27) | copy-start | bytes 2064388
  139.0 86.7 %all-reduce.6.cloned.1.call-start = ((), (), s32[]{:S(2)}) async-start(), calls=%async_computation.11 | async-start | bytes 139264 | tf_op jit(solution)/shard_map/psum | solution.py:234
  139.8 4.0 %copy-start.19 = (bf16[2688,48]{0,1:T(8,128)(2,1)S(1)}, bf16[2688,48]{0,1:T(8,128)(2,1)}, u32[]{:S(2)}) copy-start(bf16[2688,48]{0,1:T(8,128)(2,1)} %param.30) | copy-start | bytes 774148
  139.8 4.0 %copy-start.24 = (bf16[256,16]{0,1:T(8,128)(2,1)S(1)}, bf16[256,16]{0,1:T(8,128)(2,1)}, u32[]{:S(2)}) copy-start(bf16[256,16]{0,1:T(8,128)(2,1)} %copy-done.23) | copy-start | bytes 24580
  143.7 7.7 %copy-start.5 = (f32[256,256]{0,1:T(8,128)S(1)}, f32[256,256]{0,1:T(8,128)}, u32[]{:S(2)}) copy-start(f32[256,256]{0,1:T(8,128)} %copy-done.4) | copy-start | bytes 786436
  143.7 7.7 %copy-start.12 = (bf16[2688,128]{1,0:T(8,128)(2,1)S(1)}, bf16[2688,128]{1,0:T(8,128)(2,1)}, u32[]{:S(2)}) copy-start(bf16[2688,128]{1,0:T(8,128)(2,1)} %param.28) | copy-start | bytes 2064388
  143.7 156.0 %all-reduce.4.cloned.1.call-start = ((), (), s32[]{:S(2)}) async-start(), calls=%async_computation.8 | async-start | bytes 270336 | tf_op jit(solution)/shard_map/psum | solution.py:233
  151.3 158.8 %reduce-scatter.11.cloned.1.call-start = ((), (), s32[]{:S(2)}) async-start(), calls=%async_computation.7 | async-start | bytes 2064384 | tf_op jit(solution)/shard_map/reduce_scatter | solution.py:222
  155.6 154.5 %copy-start.2 = (bf16[128,2688]{1,0:T(8,128)(2,1)S(1)}, bf16[128,2688]{1,0:T(8,128)(2,1)}, u32[]{:S(2)}) copy-start(bf16[128,2688]{1,0:T(8,128)(2,1)} %param.18) | copy-start | bytes 2064388
  155.6 154.5 %copy-start.22 = (f32[2688]{0:T(1024)S(1)}, f32[2688]{0:T(1024)}, u32[]{:S(2)}) copy-start(f32[2688]{0:T(1024)} %param.22) | copy-start | bytes 32260
  155.6 154.5 %copy-start.39 = (f32[128]{0:T(128)S(1)}, f32[128]{0:T(128)}, u32[]{:S(2)}) copy-start(f32[128]{0:T(128)} %copy-done.38) | copy-start | bytes 1540
  310.1 1.6 copy-start.10
  (1 other events, 0.5 us)
Sparse Core Ops, SparseCore 0:
  11.5 12.2 all-gather.2
  54.6 11.7 reduce-scatter.12
  68.6 9.9 reduce-scatter.8
  82.3 10.7 all-gather.4
  139.1 10.3 reduce-scatter.14
  154.5 71.0 all-reduce.5
  230.0 69.7 all-reduce.3
  302.0 8.0 reduce-scatter.10
where the time goes:
time: 321 us; the launch traced here: 320 us
  waiting for transfers between devices  188 us (59%)
  matrix products  51.8 us (16%)
  starting transfers between devices  30.5 us (10%)
  other arithmetic  20.1 us (6%)
  between operations  15.6 us (5%)
  local copies, waits for them, and re-layouts  9.76 us (3%)
  blocking collectives  3.64 us (1%)
    psum x1, waiting for transfers between devices, on_device(): lax.psum(query_up_contribution.astype(jnp.bfloat16), 'ctx')  70 us
    psum x1, waiting for transfers between devices, on_device(): lax.psum(down_term, 'ctx').astype(jnp.float32)  67.5 us
    ppermute x12, starting transfers between devices, passed_along(): lax.ppermute(value, axis, [(source, source + steps) for source in range(l...  30.2 us
    dot_general x10, matrix products, multiply_by_transpose(): lax.dot_general(first_op, second_op, (((1,), (1,)), ((), ())), preferred_...  16.7 us
    ppermute x12, waiting for transfers between devices, passed_along(): lax.ppermute(value, axis, [(source, source + steps) for source in range(l...  13.4 us
    unnamed x10, waiting for transfers between devices  12.5 us
    reduce_scatter x1, waiting for transfers between devices, on_device(): lax.psum_scatter(part_out.astype(jnp.bfloat16), 'tp', scatter_dimension=0...  12.3 us
    unnamed x102, local copies, waits for them, and re-layouts  9.72 us
  transfers between devices with their start and end apart: 20, of which 10 were waited for; matrix products, arithmetic and copies ran while one was open for 10% of the time, Pallas kernels for 0%

commit v1 on v0

--- a/solution.py
+++ b/solution.py
@@ -7,6 +7,7 @@
 epsilon = 1e-06
 adapter_scale = 2.0
 score_scale = 168.0 ** (-0.5)
+lanes_note = lambda inputs, device_axis: jnp.sum(lax.all_gather(inputs, device_axis), axis=0)
 
 
 def passed_along(value, axis, steps):
@@ -230,7 +231,7 @@
         tiled=True,
     )
     adapter_totals = (
-        lax.psum(down_term, "ctx").astype(jnp.float32),
+        lanes_note(down_term, "ctx").astype(jnp.float32),
         lax.psum(query_up_contribution.astype(jnp.bfloat16), "ctx").astype(jnp.float32),
         lax.psum(key_up_contribution.astype(jnp.bfloat16), "ctx").astype(jnp.float32),
         lax.psum(value_up_contribution.astype(jnp.bfloat16), "ctx").astype(jnp.float32),

time: 321 us -> 273 us (0.85)
  waiting for transfers between devices: 188 us -> 110 us
  blocking collectives: 3.64 us -> 39.2 us
  matrix products: 51.8 us -> 48 us
    psum x1 -> x0, waiting for transfers between devices: 67.5 us -> none  [on_device(): lax.psum(down_term, 'ctx').astype(jnp.float32)]
    all_gather x0 -> x1, blocking collectives: none -> 35.5 us  [lax.all_gather(inputs, device_axis)]
    reduce_scatter x1, waiting for transfers between devices: 8.71 us -> 0.01 us  [on_device(): lax.psum_scatter(grad_normed.astype(jnp.bfloat16), 'tp', scatter_dimensio...]
    unnamed x102 -> x98, local copies, waits for them, and re-layouts: 9.72 us -> 8.45 us
    unnamed x10 -> x9, waiting for transfers between devices: 12.5 us -> 13.3 us
  transfers between devices with their start and end apart: 20 -> 19, of which waited for: 10 -> 8; matrix products, arithmetic and copies ran while one was open for 10% -> 9% of each run, Pallas kernels for 0% -> 0%
where the time goes in v1:
time: 273 us; the launch traced here: 272 us
  waiting for transfers between devices  110 us (40%)
  matrix products  48 us (18%)
  blocking collectives  39.2 us (14%)
  starting transfers between devices  30.5 us (11%)
  other arithmetic  20.6 us (8%)
  between operations  15.6 us (6%)
  local copies, waits for them, and re-layouts  8.49 us (3%)
    psum x1, waiting for transfers between devices, on_device(): lax.psum(query_up_contribution.astype(jnp.bfloat16), 'ctx')  67 us
    all_gather x1, blocking collectives, lax.all_gather(inputs, device_axis)  35.5 us
    ppermute x12, starting transfers between devices, passed_along(): lax.ppermute(value, axis, [(source, source + steps) for source in range(l...  30.2 us
    dot_general x10, matrix products, multiply_by_transpose(): lax.dot_general(first_op, second_op, (((1,), (1,)), ((), ())), preferred_...  13.6 us
    ppermute x12, waiting for transfers between devices, passed_along(): lax.ppermute(value, axis, [(source, source + steps) for source in range(l...  13.4 us
    unnamed x9, waiting for transfers between devices  13.3 us
    reduce_scatter x1, waiting for transfers between devices, on_device(): lax.psum_scatter(part_out.astype(jnp.bfloat16), 'tp', scatter_dimension=0...  12.3 us
    dot_general x10, matrix products, matrix_product(): return jnp.dot(first_op, second_op, preferred_element_type=jnp.float32)  9.23 us
  transfers between devices with their start and end apart: 19, of which 8 were waited for; matrix products, arithmetic and copies ran while one was open for 9% of the time, Pallas kernels for 0%

profile of v1, /device:TPU:0, one launch (start us, length us, event | category | flops | bytes accessed | tf_op | source)
XLA Modules:
  0.0 272.2 jit_solution(12515186945032035979)
XLA Ops:
  7.2 1.4 fusion.26
  8.7 2.2 fusion.21
  11.7 5.9 %collective-permute-start.4 = (s32[256]{0:T(256)S(1)}, s32[256]{0:T(256)S(1)}, u32[]{:S(2)}, u32[]{:S(2)}) collective-permute-start(s32[256]{0:T(256)S(1)} %get-tuple-element.19), channel_id=1, source_target_pairs={{0,8},{2,10},{4,12},{6,14},{1,9},{3,11},{5,13},{7,15},{16,24},{18,... | collective-permute-start | bytes 3080 | tf_op jit(solution)/shard_map/ppermute | solution.py:16
  17.6 4.4 %collective-permute-start.5 = (s32[256]{0:T(256)S(1)}, s32[256]{0:T(256)S(1)}, u32[]{:S(2)}, u32[]{:S(2)}) collective-permute-start(s32[256]{0:T(256)S(1)} %get-tuple-element.19), channel_id=1, source_target_pairs={{0,6},{2,8},{4,10},{6,12},{8,14},{1,7},{3,9},{5,11},{7,13},{9,15},... | collective-permute-start | bytes 3080 | tf_op jit(solution)/shard_map/ppermute | solution.py:16
  22.0 1.3 collective-permute-start.6
  23.3 3.1 %collective-permute-start.7 = (s32[256]{0:T(256)S(1)}, s32[256]{0:T(256)S(1)}, u32[]{:S(2)}, u32[]{:S(2)}) collective-permute-start(s32[256]{0:T(256)S(1)} %get-tuple-element.19), channel_id=1, source_target_pairs={{0,2},{2,4},{4,6},{6,8},{8,10},{10,12},{12,14},{1,3},{3,5},{5,7},{... | collective-permute-start | bytes 3080 | tf_op jit(solution)/shard_map/ppermute | solution.py:16
  26.5 1.2 collective-permute-done.7
  27.7 1.3 fusion.35
  29.0 2.0 convolution_convert_fusion.2
  32.9 3.9 %collective-permute-start = (bf16[256,256]{0,1:T(8,128)(2,1)S(1)}, bf16[256,256]{0,1:T(8,128)(2,1)S(1)}, u32[]{:S(2)}, u32[]{:S(2)}) collective-permute-start(bf16[256,256]{0,1:T(8,128)(2,1)S(1)} %pad_maximum_fusion.1), channel_id=1, source_target_pairs={{0,8},{2,10},{4,12},{6,14},{1,9},{3,11},{5,13},{7,15},{16,24},{18,... | collective-permute-start | bytes 393224 | tf_op jit(solution)/shard_map/ppermute | solution.py:16
  36.9 1.3 collective-permute-start.1
  38.2 1.9 collective-permute-start.2
  40.0 2.8 %collective-permute-start.3 = (bf16[256,256]{0,1:T(8,128)(2,1)S(1)}, bf16[256,256]{0,1:T(8,128)(2,1)S(1)}, u32[]{:S(2)}, u32[]{:S(2)}) collective-permute-start(bf16[256,256]{0,1:T(8,128)(2,1)S(1)} %pad_maximum_fusion.1), channel_id=1, source_target_pairs={{0,2},{2,4},{4,6},{6,8},{8,10},{10,12},{12,14},{1,3},{3,5},{5,7},{... | collective-permute-start | bytes 393224 | tf_op jit(solution)/shard_map/ppermute | solution.py:16
  43.9 0.7 constant_dynamic-update-slice_fusion.4
  45.2 0.7 constant_dynamic-update-slice_fusion.2
  45.9 0.7 constant_dynamic-update-slice_fusion.1
  47.3 3.4 %fusion.31 = f32[2,256,1280]{1,2,0:T(8,128)} fusion(pred[256,1280]{0,1:T(8,128)(4,1)S(1)} %copy-done.21, bf16[1280,256]{0,1:T(8,128)(2,1)} %constant_dynamic-update-slice_fusion, f32[256,256]{0,1:T(8,128)S(1)} %get-tuple-element.24, f32[128]{0:T(128)S(1)} %copy-done.41, f32[256,2]{0,1:T(2,128)S(1)} %add_rsqrt_fusion), kind=kOutput, calls=%fused_computation.49 | convolution fusion | flops 169936640 | bytes 3541504 | tf_op jit(solution)/shard_map/div | solution.py:129
  50.7 2.2 fusion.46
  53.1 0.8 copy.52
  54.0 3.0 %convolution_convert_fusion = bf16[256,2688]{1,0:T(8,128)(2,1)} fusion(bf16[256,256]{0,1:T(8,128)(2,1)S(1)} %bitcast.91, bf16[256,2688]{1,0:T(8,128)(2,1)} %param.29), kind=kOutput, calls=%fused_computation.4 | convolution fusion | flops 353009664 | bytes 2883584 | tf_op jit(solution)/shard_map/dot_general | solution.py:32
  57.0 8.8 %reduce-scatter.13.cloned.1.call-done = bf16[128,16]{1,0:T(8,128)(2,1)} async-done(((bf16[256,16]{1,0:T(8,128)(2,1)}), bf16[128,16]{1,0:T(8,128)(2,1)}) %reduce-scatter.13.cloned.1.call-update) | async-done | bytes 4112
  65.8 12.3 %reduce-scatter.9.cloned.1.call-done = bf16[128,2688]{1,0:T(8,128)(2,1)} async-done(((bf16[256,2688]{1,0:T(8,128)(2,1)}), bf16[128,2688]{1,0:T(8,128)(2,1)}) %reduce-scatter.9.cloned.1.call-update) | async-done | bytes 688144 | tf_op jit(solution)/shard_map/reduce_scatter | solution.py:142
  78.1 1.6 multiply_reduce_fusion.2
  80.1 1.5 multiply_convert_fusion
  81.7 0.8 copy.53
  82.5 1.8 all_gather.23
  84.3 1.4 fusion.52
  85.7 1.9 all_gather.20
  87.5 0.8 convolution_convert_fusion.4
  88.6 4.0 %all-gather.7.cloned.1.call-done = bf16[256,2688]{1,0:T(8,128)(2,1)} async-done(((bf16[128,2688]{1,0:T(8,128)(2,1)}), bf16[256,2688]{1,0:T(8,128)(2,1)}) %all-gather.7.cloned.1.call-update) | async-done | bytes 1376272 | tf_op jit(solution)/shard_map/all_gather | solution.py:159
  92.6 2.3 fusion.45
  94.9 3.2 %convolution_bitcast_fusion = f32[2,256,1280]{1,2,0:T(8,128)} fusion(bf16[256,2,128]{0,2,1:T(8,128)(2,1)S(1)} %bitcast.96, bf16[1280,256]{0,1:T(8,128)(2,1)} %constant_dynamic-update-slice_fusion), kind=kOutput, calls=%fused_computation.13 | convolution fusion | flops 167772160 | bytes 3080192 | tf_op jit(solution)/shard_map/thd,sd->hts/dot_general | solution.py:173
  98.8 5.7 %multiply_reduce_fusion.3 = (f32[256,2]{0,1:T(2,128)S(1)}, f32[256,2,128]{0,2,1:T(8,128)}) fusion(f32[256,256]{0,1:T(8,128)} %copy-done.18, f32[256,2]{0,1:T(2,128)S(1)} %copy-done.35, f32[128]{0:T(128)S(1)} %copy-done.42, f32[2,256,1280]{1,2,0:T(8,128)} %fusion.31, f32[2,256,1280]{1,2,0:T(8,128)} %convolution_bitcast_fusion, ...), kind=kOutput, calls=%fused_computation.99 | convolution fusion | flops 171312384 | bytes 11342336 | tf_op jit(solution)/shard_map/hts,sd->thd/dot_general | solution.py:178
  104.4 5.7 %convolution_bitcast_fusion.2 = f32[1280,128]{0,1:T(8,128)} fusion(f32[2,256,1280]{1,2,0:T(8,128)} %fusion.31, f32[2,256,1280]{1,2,0:T(8,128)} %convolution_bitcast_fusion, f32[256,256]{0,1:T(8,128)} %copy-done.18, f32[128]{0:T(128)S(1)} %copy-done.42, f32[256,2]{0,1:T(2,128)S(1)} %copy-done.35), kind=kOutput, calls=%fused_computation.19 | convolution fusion | flops 171247360 | bytes 6162944 | tf_op jit(solution)/shard_map/hts,thd->sd/dot_general | solution.py:181
  110.2 1.1 multiply_convert_fusion.2
  111.3 0.8 fusion.48
  112.2 2.1 fusion.83
  114.5 1.4 collective-permute-start.10
  115.9 1.3 collective-permute-start.11
  117.2 1.3 collective-permute-start.8
  118.5 1.6 collective-permute-start.9
  120.1 1.0 fusion.12
  121.2 2.0 collective-permute-done.10
  123.2 10.1 %collective-permute-done.11 = bf16[256,256]{0,1:T(8,128)(2,1)S(1)} collective-permute-done((bf16[256,256]{0,1:T(8,128)(2,1)S(1)}, bf16[256,256]{0,1:T(8,128)(2,1)S(1)}, u32[]{:S(2)}, u32[]{:S(2)}) %collective-permute-start.11) | collective-permute-done | bytes 131104 | tf_op jit(solution)/shard_map/ppermute | solution.py:16
  133.6 0.7 fusion.54
  134.4 0.7 fusion.53
  135.3 1.0 fusion.51
  136.4 4.1 %convolution_add_fusion.1 = f32[256,2688]{1,0:T(8,128)} fusion(f32[256,2688]{1,0:T(8,128)} %fusion.83, bf16[256,128]{0,1:T(8,128)(2,1)S(1)} %multiply_convert_fusion.4, bf16[2688,128]{1,0:T(8,128)(2,1)} %param.27), kind=kOutput, calls=%fused_computation.2 | convolution fusion | flops 176848896 | bytes 6258688 | tf_op jit(solution)/shard_map/dot_general | solution.py:36
  140.9 1.1 copy.54
  143.2 0.9 copy-done.3
  144.1 1.6 fusion.2
  145.8 67.0 %all-reduce.3.cloned.1.call-done = (bf16[16,256]{1,0:T(8,128)(2,1)}, bf16[16,128]{1,0:T(8,128)(2,1)}, bf16[16,128]{1,0:T(8,128)(2,1)}, bf16[256,16]{0,1:T(8,128)(2,1)}, bf16[16,1344]{1,0:T(8,128)(2,1)}) async-done(((bf16[16,256]{1,0:T(8,128)(2,1)}, bf16[16,128]{1,0:T(8,128)(2,1)}, bf16[16,128]{1,0:T(8,128)(2,1)}, bf16[256,16]{0,1:T(8,128)(2,1)}, bf16[16,1344]{1,0:T(8,128)(2,1)}), ...) | async-done | bytes 67600 | tf_op jit(solution)/shard_map/psum | solution.py:235
  212.8 1.4 convert_element_type.181
  214.2 1.3 convert_element_type.173
  215.5 1.3 convert_element_type.179
  216.8 1.3 convert_element_type.175
  218.1 1.3 convert_element_type.177
  219.3 4.3 %reduce-scatter.15.cloned.1.call-done = bf16[1344,48]{1,0:T(8,128)(2,1)} async-done(((bf16[2688,48]{1,0:T(8,128)(2,1)}), bf16[1344,48]{1,0:T(8,128)(2,1)}) %reduce-scatter.15.cloned.1.call-update) | async-done | bytes 129040
  223.7 1.1 copy.55
  224.8 35.5 %all-gather.1 = bf16[8,1344,48]{1,2,0:T(8,128)(2,1)} all-gather(bf16[1,1344,48]{1,2,0:T(8,128)(2,1)S(1)} %bitcast.98), channel_id=2, replica_groups=mesh['groups'=2,'ctx'=8,'tp'=2] {'ctx'}, dimensions={0}, use_global_device_ids=true | all-gather | bytes 1161216 | tf_op jit(solution)/shard_map/all_gather | solution.py:10
  260.4 1.4 reduce_sum.128
  261.8 0.7 convert_element_type.171
  262.5 1.6 fusion.22
  264.1 1.3 fusion.25
  (150 shorter events, 8.2 us)
Async XLA Ops:
  7.2 35.9 %copy-start = (bf16[2688,256]{1,0:T(8,128)(2,1)S(1)}, bf16[2688,256]{1,0:T(8,128)(2,1)}, u32[]{:S(2)}) copy-start(bf16[2688,256]{1,0:T(8,128)(2,1)} %param.26) | copy-start | bytes 4128772
  7.2 4.5 %copy-start.40 = (s32[256]{0:T(256)S(1)}, s32[256]{0:T(256)}, u32[]{:S(2)}) copy-start(s32[256]{0:T(256)} %param.20) | copy-start | bytes 3076
  7.2 21.8 %all-gather.5.cloned.1.call-start = ((), (), s32[]{:S(2)}) async-start(), calls=%async_computation.4 | async-start | bytes 2064384 | tf_op jit(solution)/shard_map/all_gather | solution.py:89
  8.7 20.3 %copy-start.36 = (f32[128]{0:T(128)}, f32[128]{0:T(128)S(1)}, u32[]{:S(2)}) copy-start(f32[128]{0:T(128)S(1)} %add_rsqrt_fusion.3) | copy-start | bytes 1540
  10.8 20.2 %copy-start.28 = (bf16[16,128]{1,0:T(8,128)(2,1)S(1)}, bf16[16,128]{1,0:T(8,128)(2,1)}, u32[]{:S(2)}) copy-start(bf16[16,128]{1,0:T(8,128)(2,1)} %param.32) | copy-start | bytes 12292
  10.9 20.4 %copy-start.8 = (bf16[2688,128]{1,0:T(8,128)(2,1)S(1)}, bf16[2688,128]{1,0:T(8,128)(2,1)}, u32[]{:S(2)}) copy-start(bf16[2688,128]{1,0:T(8,128)(2,1)} %param.27) | copy-start | bytes 2064388
  10.9 55.0 %reduce-scatter.13.cloned.1.call-start = ((), (), s32[]{:S(2)}) async-start(), calls=%async_computation.8 | async-start | bytes 98304
  11.7 14.8 %collective-permute-start.4 = (s32[256]{0:T(256)S(1)}, s32[256]{0:T(256)S(1)}, u32[]{:S(2)}, u32[]{:S(2)}) collective-permute-start(s32[256]{0:T(256)S(1)} %get-tuple-element.19), channel_id=1, source_target_pairs={{0,8},{2,10},{4,12},{6,14},{1,9},{3,11},{5,13},{7,15},{16,24},{18,... | collective-permute-start | bytes 3080 | tf_op jit(solution)/shard_map/ppermute | solution.py:16
  17.6 8.9 %collective-permute-start.5 = (s32[256]{0:T(256)S(1)}, s32[256]{0:T(256)S(1)}, u32[]{:S(2)}, u32[]{:S(2)}) collective-permute-start(s32[256]{0:T(256)S(1)} %get-tuple-element.19), channel_id=1, source_target_pairs={{0,6},{2,8},{4,10},{6,12},{8,14},{1,7},{3,9},{5,11},{7,13},{9,15},... | collective-permute-start | bytes 3080 | tf_op jit(solution)/shard_map/ppermute | solution.py:16
  22.0 4.5 %collective-permute-start.6 = (s32[256]{0:T(256)S(1)}, s32[256]{0:T(256)S(1)}, u32[]{:S(2)}, u32[]{:S(2)}) collective-permute-start(s32[256]{0:T(256)S(1)} %get-tuple-element.19), channel_id=1, source_target_pairs={{0,4},{2,6},{4,8},{6,10},{8,12},{10,14},{1,5},{3,7},{5,9},{7,11},{... | collective-permute-start | bytes 3080 | tf_op jit(solution)/shard_map/ppermute | solution.py:16
  23.3 4.4 %collective-permute-start.7 = (s32[256]{0:T(256)S(1)}, s32[256]{0:T(256)S(1)}, u32[]{:S(2)}, u32[]{:S(2)}) collective-permute-start(s32[256]{0:T(256)S(1)} %get-tuple-element.19), channel_id=1, source_target_pairs={{0,2},{2,4},{4,6},{6,8},{8,10},{10,12},{12,14},{1,3},{3,5},{5,7},{... | collective-permute-start | bytes 3080 | tf_op jit(solution)/shard_map/ppermute | solution.py:16
  26.4 24.3 %copy-start.32 = (f32[256]{0:T(256)}, f32[256]{0:T(256)S(1)}, u32[]{:S(2)}) copy-start(f32[256]{0:T(256)S(1)} %fusion.70) | copy-start | bytes 3076
  29.0 2.3 copy-start.1
  31.0 0.9 copy-start.30
  31.0 1.2 copy-start.38
  31.0 1.2 copy-start.11
  31.9 1.0 copy-start.14
  32.2 10.7 %copy-start.26 = (bf16[16,256]{1,0:T(8,128)(2,1)S(1)}, bf16[16,256]{1,0:T(8,128)(2,1)}, u32[]{:S(2)}) copy-start(bf16[16,256]{1,0:T(8,128)(2,1)} %param.31) | copy-start | bytes 24580
  32.9 10.9 %collective-permute-start = (bf16[256,256]{0,1:T(8,128)(2,1)S(1)}, bf16[256,256]{0,1:T(8,128)(2,1)S(1)}, u32[]{:S(2)}, u32[]{:S(2)}) collective-permute-start(bf16[256,256]{0,1:T(8,128)(2,1)S(1)} %pad_maximum_fusion.1), channel_id=1, source_target_pairs={{0,8},{2,10},{4,12},{6,14},{1,9},{3,11},{5,13},{7,15},{16,24},{18,... | collective-permute-start | bytes 393224 | tf_op jit(solution)/shard_map/ppermute | solution.py:16
  36.9 7.7 %collective-permute-start.1 = (bf16[256,256]{0,1:T(8,128)(2,1)S(1)}, bf16[256,256]{0,1:T(8,128)(2,1)S(1)}, u32[]{:S(2)}, u32[]{:S(2)}) collective-permute-start(bf16[256,256]{0,1:T(8,128)(2,1)S(1)} %pad_maximum_fusion.1), channel_id=1, source_target_pairs={{0,6},{2,8},{4,10},{6,12},{8,14},{1,7},{3,9},{5,11},{7,13},{9,15},... | collective-permute-start | bytes 393224 | tf_op jit(solution)/shard_map/ppermute | solution.py:16
  38.2 7.1 %collective-permute-start.2 = (bf16[256,256]{0,1:T(8,128)(2,1)S(1)}, bf16[256,256]{0,1:T(8,128)(2,1)S(1)}, u32[]{:S(2)}, u32[]{:S(2)}) collective-permute-start(bf16[256,256]{0,1:T(8,128)(2,1)S(1)} %pad_maximum_fusion.1), channel_id=1, source_target_pairs={{0,4},{2,6},{4,8},{6,10},{8,12},{10,14},{1,5},{3,7},{5,9},{7,11},{... | collective-permute-start | bytes 393224 | tf_op jit(solution)/shard_map/ppermute | solution.py:16
  40.0 5.9 %collective-permute-start.3 = (bf16[256,256]{0,1:T(8,128)(2,1)S(1)}, bf16[256,256]{0,1:T(8,128)(2,1)S(1)}, u32[]{:S(2)}, u32[]{:S(2)}) collective-permute-start(bf16[256,256]{0,1:T(8,128)(2,1)S(1)} %pad_maximum_fusion.1), channel_id=1, source_target_pairs={{0,2},{2,4},{4,6},{6,8},{8,10},{10,12},{12,14},{1,3},{3,5},{5,7},{... | collective-permute-start | bytes 393224 | tf_op jit(solution)/shard_map/ppermute | solution.py:16
  43.1 4.2 %copy-start.21 = (pred[256,1280]{0,1:T(8,128)(4,1)S(1)}, pred[256,1280]{0,1:T(8,128)(4,1)}, u32[]{:S(2)}) copy-start(pred[256,1280]{0,1:T(8,128)(4,1)} %fusion.35) | copy-start | bytes 983044
  43.1 4.2 %copy-start.41 = (f32[128]{0:T(128)S(1)}, f32[128]{0:T(128)}, u32[]{:S(2)}) copy-start(f32[128]{0:T(128)} %param.23) | copy-start | bytes 1540
  43.8 3.5 %copy-start.18 = (f32[256,256]{0,1:T(8,128)}, f32[256,256]{0,1:T(8,128)S(1)}, u32[]{:S(2)}) copy-start(f32[256,256]{0,1:T(8,128)S(1)} %get-tuple-element.24) | copy-start | bytes 786436
  43.8 6.9 %copy-start.34 = (f32[256,2]{0,1:T(2,128)}, f32[256,2]{0,1:T(2,128)S(1)}, u32[]{:S(2)}) copy-start(f32[256,2]{0,1:T(2,128)S(1)} %add_rsqrt_fusion) | copy-start | bytes 6148
  50.7 2.2 copy-start.24
  53.0 4.0 %copy-start.16 = (bf16[128,2,256]{2,0,1:T(8,128)(2,1)}, bf16[128,2,256]{2,0,1:T(8,128)(2,1)S(1)}, u32[]{:S(2)}) copy-start(bf16[128,2,256]{2,0,1:T(8,128)(2,1)S(1)} %fusion.46) | copy-start | bytes 393220
  53.9 24.2 %reduce-scatter.9.cloned.1.call-start = ((), (), s32[]{:S(2)}) async-start(), calls=%async_computation.5 | async-start | bytes 2064384 | tf_op jit(solution)/shard_map/reduce_scatter | solution.py:142
  57.0 21.2 %copy-start.20 = (bf16[16,2688]{1,0:T(8,128)(2,1)S(1)}, bf16[16,2688]{1,0:T(8,128)(2,1)}, u32[]{:S(2)}) copy-start(bf16[16,2688]{1,0:T(8,128)(2,1)} %param.35) | copy-start | bytes 258052
  57.0 22.7 %copy-start.9 = (bf16[128,2688]{1,0:T(8,128)(2,1)S(1)}, bf16[128,2688]{1,0:T(8,128)(2,1)}, u32[]{:S(2)}) copy-start(bf16[128,2688]{1,0:T(8,128)(2,1)} %param.19) | copy-start | bytes 2064388
  57.0 35.6 %all-gather.7.cloned.1.call-start = ((), (), s32[]{:S(2)}) async-start(), calls=%async_computation.6 | async-start | bytes 2064384 | tf_op jit(solution)/shard_map/all_gather | solution.py:159
  78.1 1.6 copy-start.23
  81.6 5.9 %copy-start.17 = (bf16[128,2,256]{2,0,1:T(8,128)(2,1)S(1)}, bf16[128,2,256]{2,0,1:T(8,128)(2,1)}, u32[]{:S(2)}) copy-start(bf16[128,2,256]{2,0,1:T(8,128)(2,1)} %copy-done.16) | copy-start | bytes 393220
  81.6 6.7 %copy-start.25 = (bf16[256,16]{0,1:T(8,128)(2,1)S(1)}, bf16[256,16]{0,1:T(8,128)(2,1)}, u32[]{:S(2)}) copy-start(bf16[256,16]{0,1:T(8,128)(2,1)} %param.34) | copy-start | bytes 24580
  81.6 10.9 %copy-start.33 = (f32[256]{0:T(256)S(1)}, f32[256]{0:T(256)}, u32[]{:S(2)}) copy-start(f32[256]{0:T(256)} %copy-done.32) | copy-start | bytes 3076
  81.7 131.1 %all-reduce.3.cloned.1.call-start = ((), (), s32[]{:S(2)}) async-start(), calls=%async_computation.10 | async-start | bytes 139264 | tf_op jit(solution)/shard_map/psum | solution.py:235
  94.9 3.2 %copy-start.4 = (f32[2,256,1280]{1,2,0:T(8,128)S(1)}, f32[2,256,1280]{1,2,0:T(8,128)}, u32[]{:S(2)}) copy-start(f32[2,256,1280]{1,2,0:T(8,128)} %fusion.31) | copy-start | bytes 7864324
  98.1 0.7 copy-start.35
  98.1 0.7 copy-start.42
  104.4 7.6 %copy-start.27 = (bf16[16,256]{1,0:T(8,128)(2,1)S(1)}, bf16[16,256]{1,0:T(8,128)(2,1)}, u32[]{:S(2)}) copy-start(bf16[16,256]{1,0:T(8,128)(2,1)} %param.31) | copy-start | bytes 24580
  112.2 2.1 copy-start.13
  114.3 5.8 %copy-start.7 = (bf16[256,2688]{1,0:T(8,128)(2,1)S(1)}, bf16[256,2688]{1,0:T(8,128)(2,1)}, u32[]{:S(2)}) copy-start(bf16[256,2688]{1,0:T(8,128)(2,1)} %all-gather.7.cloned.1.call-done) | copy-start | bytes 4128772
  114.5 8.7 %collective-permute-start.10 = (bf16[256,256]{0,1:T(8,128)(2,1)S(1)}, bf16[256,256]{0,1:T(8,128)(2,1)S(1)}, u32[]{:S(2)}, u32[]{:S(2)}) collective-permute-start(bf16[256,256]{0,1:T(8,128)(2,1)S(1)} %get-tuple-element.17), channel_id=1, source_target_pairs={{6,0},{8,2},{10,4},{12,6},{14,8},{7,1},{9,3},{11,5},{13,7},{15,9},... | collective-permute-start | bytes 393224 | tf_op jit(solution)/shard_map/ppermute | solution.py:16
  115.9 17.4 %collective-permute-start.11 = (bf16[256,256]{0,1:T(8,128)(2,1)S(1)}, bf16[256,256]{0,1:T(8,128)(2,1)S(1)}, u32[]{:S(2)}, u32[]{:S(2)}) collective-permute-start(bf16[256,256]{0,1:T(8,128)(2,1)S(1)} %get-tuple-element.16), channel_id=1, source_target_pairs={{8,0},{10,2},{12,4},{14,6},{9,1},{11,3},{13,5},{15,7},{24,16},{26,... | collective-permute-start | bytes 393224 | tf_op jit(solution)/shard_map/ppermute | solution.py:16
  117.2 16.1 %collective-permute-start.8 = (bf16[256,256]{0,1:T(8,128)(2,1)S(1)}, bf16[256,256]{0,1:T(8,128)(2,1)S(1)}, u32[]{:S(2)}, u32[]{:S(2)}) collective-permute-start(bf16[256,256]{0,1:T(8,128)(2,1)S(1)} %get-tuple-element.15), channel_id=1, source_target_pairs={{2,0},{4,2},{6,4},{8,6},{10,8},{12,10},{14,12},{3,1},{5,3},{7,5},{... | collective-permute-start | bytes 393224 | tf_op jit(solution)/shard_map/ppermute | solution.py:16
  118.5 14.9 %copy-start.15 = (f32[256,128]{0,1:T(8,128)S(1)}, f32[256,128]{0,1:T(8,128)}, u32[]{:S(2)}) copy-start(f32[256,128]{0,1:T(8,128)} %copy-done.14) | copy-start | bytes 393220
  118.5 14.9 %copy-start.39 = (f32[128]{0:T(128)S(1)}, f32[128]{0:T(128)}, u32[]{:S(2)}) copy-start(f32[128]{0:T(128)} %param.24) | copy-start | bytes 1540
  118.5 14.8 %collective-permute-start.9 = (bf16[256,256]{0,1:T(8,128)(2,1)S(1)}, bf16[256,256]{0,1:T(8,128)(2,1)S(1)}, u32[]{:S(2)}, u32[]{:S(2)}) collective-permute-start(bf16[256,256]{0,1:T(8,128)(2,1)S(1)} %get-tuple-element.18), channel_id=1, source_target_pairs={{4,0},{6,2},{8,4},{10,6},{12,8},{14,10},{5,1},{7,3},{9,5},{11,7},{... | collective-permute-start | bytes 393224 | tf_op jit(solution)/shard_map/ppermute | solution.py:16
  121.2 14.0 %copy-start.29 = (bf16[16,128]{1,0:T(8,128)(2,1)S(1)}, bf16[16,128]{1,0:T(8,128)(2,1)}, u32[]{:S(2)}) copy-start(bf16[16,128]{1,0:T(8,128)(2,1)} %param.32) | copy-start | bytes 12292
  121.2 14.1 %copy-start.31 = (bf16[16,128]{1,0:T(8,128)(2,1)S(1)}, bf16[16,128]{1,0:T(8,128)(2,1)}, u32[]{:S(2)}) copy-start(bf16[16,128]{1,0:T(8,128)(2,1)} %param.33) | copy-start | bytes 12292
  133.5 0.9 copy-start.5
  140.4 1.7 copy-start.19
  140.5 83.2 %reduce-scatter.15.cloned.1.call-start = ((), (), s32[]{:S(2)}) async-start(), calls=%async_computation.9 | async-start | bytes 1032192
  142.0 1.1 copy-start.12
  142.0 1.1 copy-start.6
  142.0 120.5 %reduce-scatter.11.cloned.1.call-start = ((), (), s32[]{:S(2)}) async-start(), calls=%async_computation.7 | async-start | bytes 2064384 | tf_op jit(solution)/shard_map/reduce_scatter | solution.py:223
  142.1 2.0 copy-start.3
  224.8 37.7 %copy-start.2 = (bf16[128,2688]{1,0:T(8,128)(2,1)S(1)}, bf16[128,2688]{1,0:T(8,128)(2,1)}, u32[]{:S(2)}) copy-start(bf16[128,2688]{1,0:T(8,128)(2,1)} %param.18) | copy-start | bytes 2064388
  224.8 37.7 %copy-start.22 = (f32[2688]{0:T(1024)S(1)}, f32[2688]{0:T(1024)}, u32[]{:S(2)}) copy-start(f32[2688]{0:T(1024)} %param.22) | copy-start | bytes 32260
  224.8 37.7 %copy-start.37 = (f32[128]{0:T(128)S(1)}, f32[128]{0:T(128)}, u32[]{:S(2)}) copy-start(f32[128]{0:T(128)} %copy-done.36) | copy-start | bytes 1540
  262.5 1.6 copy-start.10
Sparse Core Ops, SparseCore 0:
  11.0 12.2 all-gather.4
  54.0 11.7 reduce-scatter.12
  68.1 9.9 reduce-scatter.8
  81.8 10.7 all-gather.6
  140.6 72.1 all-reduce.2
  215.5 8.0 reduce-scatter.14
  226.0 9.9 reduce-scatter.10
